TPU v7x, 128 devices: a whole 4x4x4 slice. The times are simulated.
128 devices in a mesh: grp: 16 (over y, z), lag: 8 (over x, core).
Axes of the slice: x: 4, y: 4, z: 4, core: 2. Of those that a mesh axis runs over, the one named last changes fastest.
Arguments:
- history: float32 [16, 512, 32, 128], P('lag', 'grp'), may hold values from -6 to 6
- tiles: bfloat16 [65536, 128, 128], P(('grp', 'lag')), may hold values from -0.01171875 to 0.01171875
- tile_src: int32 [65536], P(('grp', 'lag')), may hold values from 0 to 511
- tile_obs: int32 [65536], P(('grp', 'lag')), may hold values from 0 to 32
- tile_lag: int32 [65536], P(('grp', 'lag')), may hold values from 0 to 1
- incident: float32 [32, 32, 128], P('grp', 'lag'), may hold values from -6 to 6
- near_inverse: bfloat16 [32, 128, 128], P('grp'), may hold values from -0.5 to 0.5
Outputs:
- field: float32 [32, 32, 128], P('grp', 'lag')
- new_current: float32 [32, 32, 128], P('grp', 'lag')
Inputs may be any that keep to these rules, and one draw needn't show every extreme that they name: `tile_obs`: a value of 32 marks a padded tile.
All inputs are finite; a program needn't handle non-finite values.
Results may differ from a plain program's by a relative error of at most 0.0035.
Values may be sent and summed in bfloat16 or wider, within the bound.
No kernel may reach another device: no remote copies, remote signals or barrier semaphores. Data moves between devices by JAX's collectives and lax.ppermute only.
A program may use at most 128 MiB of HBM per device.

v0:
```python
import jax
import jax.numpy as jnp
from jax import lax
from jax.sharding import PartitionSpec as P

OBS_DEV = 2


def body(history, tiles, tile_src, tile_obs, tile_lag, incident, near_inverse):
    hist16 = history.astype(jnp.bfloat16)
    gathered = lax.all_gather(hist16, "grp", axis=1, tiled=True)
    lag_count = gathered.shape[0]
    source_count = gathered.shape[1]
    flat = gathered.reshape(lag_count * source_count, gathered.shape[2], gathered.shape[3])
    picked = flat[tile_lag * source_count + tile_src]
    terms = jnp.einsum("kas,kos->kao", picked, tiles, preferred_element_type=jnp.float32)
    observers = OBS_DEV * lax.axis_size("grp")
    partial_field = jax.ops.segment_sum(terms, tile_obs, num_segments=observers)
    angle_part = incident.shape[1]
    summed = lax.psum(partial_field, "lag")
    mine = lax.psum_scatter(summed, "grp", scatter_dimension=0, tiled=True)
    field = lax.dynamic_slice_in_dim(mine, lax.axis_index("lag") * angle_part, angle_part, 1)
    rhs = (incident - field).astype(jnp.bfloat16)
    new_current = jnp.einsum("oag,ohg->oah", rhs, near_inverse, preferred_element_type=jnp.float32)
    return (field, new_current)


def solution(mesh):
    return jax.shard_map(
        body,
        mesh=mesh,
        in_specs=(
            P("lag", "grp", None, None),
            P(("grp", "lag"), None, None),
            P(("grp", "lag")),
            P(("grp", "lag")),
            P(("grp", "lag")),
            P("grp", "lag", None),
            P("grp", None, None),
        ),
        out_specs=(P("grp", "lag", None), P("grp", "lag", None)),
        check_vma=False,
    )
```

profile of v0, /device:TPU:0, one launch (start us, length us, event | category | flops | bytes accessed | tf_op | source)
XLA Modules:
  0.0 255.2 jit_solution(2422170448194656881)
XLA Ops:
  7.2 0.0 copy-start
  7.2 0.0 all-gather.2.cloned.1.call-start
  7.2 2.2 convert_element_type.6
  9.4 0.0 all-gather.2.cloned.1.call-update
  9.4 0.0 reduce-scatter.2.cloned.1.call-start
  9.5 0.7 compare_select_fusion
  10.2 73.4 %all-gather.2.cloned.1.call-done = bf16[2,512,32,128]{3,2,1,0:T(8,128)(2,1)} async-done(((bf16[2,32,32,128]{3,2,1,0:T(8,128)(2,1)}), bf16[2,512,32,128]{3,2,1,0:T(8,128)(2,1)}) %all-gather.2.cloned.1.call-update) | async-done | bytes 8388624 | tf_op jit(solution)/shard_map/all_gather | solution.py:11
  83.6 6.5 %gather_fusion = bf16[512,32,128]{2,1,0:T(8,128)(2,1)} fusion(bf16[1024,32,128]{2,1,0:T(8,128)(2,1)} %bitcast.4, s32[1024]{0:T(1024)S(1)} %pad_clamp_fusion), kind=kCustom, calls=%fused_computation | custom fusion | bytes 8390656 | tf_op jit(solution)/shard_map/gather | solution.py:15
  90.1 0.0 copy-start.4
  90.1 15.0 %fusion.1 = f32[512,32,128]{2,1,0:T(8,128)} fusion(bf16[512,32,128]{2,1,0:T(8,128)(2,1)} %gather_fusion, bf16[512,128,128]{2,1,0:T(8,128)(2,1)} %param.8), kind=kOutput, calls=%fused_computation.7 | convolution fusion | flops 536870912 | bytes 29360128 | tf_op jit(solution)/shard_map/kas,kos->kao/dot_general | solution.py:16
  105.2 0.0 copy-done.4
  105.2 0.0 copy-start.3
  105.2 44.7 %scatter_fusion = f32[32,32,128]{2,1,0:T(8,128)S(1)} fusion(f32[32,32,128]{2,1,0:T(8,128)S(1)} %broadcast_in_dim.9, s32[512]{0:T(512)S(1)} %copy-done.4, f32[512,32,128]{2,1,0:T(8,128)} %fusion.1), kind=kCustom, calls=%fused_computation.1 | custom fusion | flops 2097152 | bytes 25167872 | tf_op jit(solution)/shard_map/scatter-add | solution.py:18
  149.9 0.0 copy-start.1
  149.9 0.8 copy-done.1
  150.7 0.0 reduce-scatter.2.cloned.1.call-update
  150.7 72.3 %reduce-scatter.2.cloned.1.call-done = f32[2,32,128]{2,1,0:T(8,128)} async-done(((f32[32,32,128]{2,1,0:T(8,128)}), f32[2,32,128]{2,1,0:T(8,128)}) %reduce-scatter.2.cloned.1.call-update) | async-done | bytes 32784 | tf_op jit(solution)/shard_map/reduce_scatter | solution.py:21
  223.0 24.6 %psum.8 = f32[2,32,128]{2,1,0:T(8,128)S(1)} all-reduce(f32[2,32,128]{2,1,0:T(8,128)} %reduce-scatter.2.cloned.1.call-done), channel_id=1, replica_groups=mesh['grp'=16,'lag'=8] {'lag'}, use_global_device_ids=true, to_apply=%region_1.0 | all-reduce | flops 8192 | bytes 65536 | tf_op jit(solution)/shard_map/psum | solution.py:20
  247.6 0.0 copy-done
  247.6 0.0 copy-done.3
  247.6 0.0 copy-start.2
  247.6 0.7 fusion
  248.4 0.0 copy-done.2
  (3 shorter events, 0.1 us)
Async XLA Ops:
  7.2 240.4 %copy-start = (bf16[2,128,128]{2,1,0:T(8,128)(2,1)S(1)}, bf16[2,128,128]{2,1,0:T(8,128)(2,1)}, u32[]{:S(2)}) copy-start(bf16[2,128,128]{2,1,0:T(8,128)(2,1)} %param.13) | copy-start | bytes 196612
  7.2 76.4 %all-gather.2.cloned.1.call-start = ((), (), s32[]{:S(2)}) async-start(), calls=%async_computation.1 | async-start | bytes 8912896 | tf_op jit(solution)/shard_map/all_gather | solution.py:11
  9.4 213.6 %reduce-scatter.2.cloned.1.call-start = ((), (), s32[]{:S(2)}) async-start(), calls=%async_computation.2 | async-start | bytes 557056 | tf_op jit(solution)/shard_map/reduce_scatter | solution.py:21
  90.1 15.0 %copy-start.4 = (s32[512]{0:T(512)S(1)}, s32[512]{0:T(512)}, u32[]{:S(2)}) copy-start(s32[512]{0:T(512)} %param.10) | copy-start | bytes 6148
  105.2 142.4 %copy-start.3 = (f32[2,4,128]{2,1,0:T(4,128)S(1)}, f32[2,4,128]{2,1,0:T(4,128)}, u32[]{:S(2)}) copy-start(f32[2,4,128]{2,1,0:T(4,128)} %param.12) | copy-start | bytes 12292
  149.9 0.8 copy-start.1
  247.6 0.8 copy-start.2
Sparse Core Ops, SparseCore 0:
  10.2 73.3 all-gather.1
  150.8 72.1 reduce-scatter.1
where the time goes:
time: 256 us; the launch traced here: 255 us
  waiting for transfers between devices  146 us (57%)
  other arithmetic  47.6 us (19%)
  blocking collectives  24.6 us (10%)
  matrix products  15.7 us (6%)
  between operations  14.1 us (6%)
  local copies, waits for them, and re-layouts  7.41 us (3%)
    all_gather x1, waiting for transfers between devices, body(): gathered = lax.all_gather(hist16, 'grp', axis=1, tiled=True)  73.4 us
    reduce_scatter x1, waiting for transfers between devices, body(): mine = lax.psum_scatter(summed, 'grp', scatter_dimension=0, tiled=True)  72.3 us
    scatter-add x1, other arithmetic, body(): partial_field = jax.ops.segment_sum(terms, tile_obs, num_segments=observers)  44.7 us
    psum x1, blocking collectives, body(): summed = lax.psum(partial_field, 'lag')  24.6 us
    dot_general x1, matrix products, body(): jnp.einsum('kas,kos->kao', picked, tiles, preferred_element_type=jnp.floa...  15 us
    gather x1, local copies, waits for them, and re-layouts, body(): picked = flat[tile_lag * source_count + tile_src]  6.55 us
  transfers between devices with their start and end apart: 2, of which 2 were waited for; matrix products, arithmetic and copies ran while one was open for 0% of the time, Pallas kernels for 0%

commit v1 on v0

--- a/solution.py
+++ b/solution.py
@@ -7,6 +7,10 @@
 
 
 def body(history, tiles, tile_src, tile_obs, tile_lag, incident, near_inverse):
+
+    def step_on_teams(arr_in):
+        return jnp.sum(jax.lax.all_gather(arr_in, "lag"), 0)
+
     hist16 = history.astype(jnp.bfloat16)
     gathered = lax.all_gather(hist16, "grp", axis=1, tiled=True)
     lag_count = gathered.shape[0]
@@ -17,7 +21,7 @@
     observers = OBS_DEV * lax.axis_size("grp")
     partial_field = jax.ops.segment_sum(terms, tile_obs, num_segments=observers)
     angle_part = incident.shape[1]
-    summed = lax.psum(partial_field, "lag")
+    summed = step_on_teams(partial_field)
     mine = lax.psum_scatter(summed, "grp", scatter_dimension=0, tiled=True)
     field = lax.dynamic_slice_in_dim(mine, lax.axis_index("lag") * angle_part, angle_part, 1)
     rhs = (incident - field).astype(jnp.bfloat16)

time: 256 us -> 268 us (1.047)
  waiting for transfers between devices: 146 us -> 178 us
  blocking collectives: 24.6 us -> 0 us
  other arithmetic: 47.6 us -> 51.1 us
    all_gather x0 -> x1, waiting for transfers between devices: none -> 31.8 us  [step_on_teams(): return jnp.sum(jax.lax.all_gather(arr_in, 'lag'), 0)]
    psum x1 -> x0, blocking collectives: 24.6 us -> none  [body(): summed = lax.psum(partial_field, 'lag')]
    reduce_sum x0 -> x1, other arithmetic: none -> 3.5 us  [step_on_teams(): return jnp.sum(jax.lax.all_gather(arr_in, 'lag'), 0)]
  transfers between devices with their start and end apart: 2 -> 3, of which waited for: 2 -> 3; matrix products, arithmetic and copies ran while one was open for 0% -> 0% of each run, Pallas kernels for 0% -> 0%
where the time goes in v1:
time: 268 us; the launch traced here: 267 us
  waiting for transfers between devices  178 us (66%)
  other arithmetic  51.1 us (19%)
  matrix products  15.7 us (6%)
  between operations  13.8 us (5%)
  local copies, waits for them, and re-layouts  8.12 us (3%)
    all_gather x1, waiting for transfers between devices, body(): gathered = lax.all_gather(hist16, 'grp', axis=1, tiled=True)  73.4 us
    reduce_scatter x1, waiting for transfers between devices, body(): mine = lax.psum_scatter(summed, 'grp', scatter_dimension=0, tiled=True)  72.6 us
    scatter-add x1, other arithmetic, body(): partial_field = jax.ops.segment_sum(terms, tile_obs, num_segments=observers)  44.7 us
    all_gather x1, waiting for transfers between devices, step_on_teams(): return jnp.sum(jax.lax.all_gather(arr_in, 'lag'), 0)  31.8 us
    dot_general x1, matrix products, body(): jnp.einsum('kas,kos->kao', picked, tiles, preferred_element_type=jnp.floa...  15 us
    gather x1, local copies, waits for them, and re-layouts, body(): picked = flat[tile_lag * source_count + tile_src]  6.55 us
  transfers between devices with their start and end apart: 3, of which 3 were waited for; matrix products, arithmetic and copies ran while one was open for 0% of the time, Pallas kernels for 0%

profile of v1, /device:TPU:0, one launch (start us, length us, event | category | flops | bytes accessed | tf_op | source)
XLA Modules:
  0.0 266.7 jit_solution(8765162983961375980)
XLA Ops:
  7.2 0.0 copy-start
  7.2 0.0 all-gather.4.cloned.1.call-start
  7.2 2.1 convert_element_type.6
  9.4 0.0 all-gather.4.cloned.1.call-update
  9.4 0.0 all-gather.6.cloned.1.call-start
  9.4 0.7 compare_select_fusion
  10.2 73.4 %all-gather.4.cloned.1.call-done = bf16[2,512,32,128]{3,2,1,0:T(8,128)(2,1)} async-done(((bf16[2,32,32,128]{3,2,1,0:T(8,128)(2,1)}), bf16[2,512,32,128]{3,2,1,0:T(8,128)(2,1)}) %all-gather.4.cloned.1.call-update) | async-done | bytes 8388624 | tf_op jit(solution)/shard_map/all_gather | solution.py:15
  83.6 6.5 %gather_fusion = bf16[512,32,128]{2,1,0:T(8,128)(2,1)} fusion(bf16[1024,32,128]{2,1,0:T(8,128)(2,1)} %bitcast.6, s32[1024]{0:T(1024)S(1)} %pad_clamp_fusion), kind=kCustom, calls=%fused_computation | custom fusion | bytes 8390656 | tf_op jit(solution)/shard_map/gather | solution.py:19
  90.1 0.0 copy-start.4
  90.1 15.0 %fusion.1 = f32[512,32,128]{2,1,0:T(8,128)} fusion(bf16[512,32,128]{2,1,0:T(8,128)(2,1)} %gather_fusion, bf16[512,128,128]{2,1,0:T(8,128)(2,1)} %param.8), kind=kOutput, calls=%fused_computation.7 | convolution fusion | flops 536870912 | bytes 29360128 | tf_op jit(solution)/shard_map/kas,kos->kao/dot_general | solution.py:20
  105.2 0.0 copy-done.4
  105.2 0.0 copy-start.3
  105.2 44.7 %scatter_fusion = f32[32,32,128]{2,1,0:T(8,128)S(1)} fusion(f32[32,32,128]{2,1,0:T(8,128)S(1)} %broadcast_in_dim.9, s32[512]{0:T(512)S(1)} %copy-done.4, f32[512,32,128]{2,1,0:T(8,128)} %fusion.1), kind=kCustom, calls=%fused_computation.1 | custom fusion | flops 2097152 | bytes 25167872 | tf_op jit(solution)/shard_map/scatter-add | solution.py:22
  149.9 0.0 copy-start.1
  149.9 0.8 copy-done.1
  150.7 0.0 all-gather.6.cloned.1.call-update
  150.7 0.0 reduce-scatter.2.cloned.1.call-start
  150.8 31.8 %all-gather.6.cloned.1.call-done = f32[256,32,128]{2,1,0:T(8,128)} async-done(((f32[32,32,128]{2,1,0:T(8,128)}), f32[256,32,128]{2,1,0:T(8,128)}) %all-gather.6.cloned.1.call-update) | async-done | bytes 4194320 | tf_op jit(solution)/shard_map/all_gather | solution.py:12
  182.6 3.5 %reduce_sum.9 = f32[32,32,128]{2,1,0:T(8,128)} reduce(f32[8,32,32,128]{3,2,1,0:T(8,128)} %bitcast.5, f32[]{:T(128)} %constant.7.clone.1), dimensions={0}, to_apply=%region_1.0 | reduce | flops 917504 | bytes 4718596 | tf_op jit(solution)/shard_map/reduce_sum | solution.py:12
  186.1 0.0 reduce-scatter.2.cloned.1.call-update
  186.1 72.6 %reduce-scatter.2.cloned.1.call-done = f32[2,32,128]{2,1,0:T(8,128)} async-done(((f32[32,32,128]{2,1,0:T(8,128)}), f32[2,32,128]{2,1,0:T(8,128)}) %reduce-scatter.2.cloned.1.call-update) | async-done | bytes 32784 | tf_op jit(solution)/shard_map/reduce_scatter | solution.py:25
  258.7 0.7 constant_dynamic-slice_fusion
  259.4 0.0 copy-done
  259.4 0.0 copy-done.3
  259.4 0.0 copy-start.2
  259.4 0.7 fusion
  260.1 0.0 copy-done.2
  (2 shorter events, 0.1 us)
Async XLA Ops:
  7.2 252.2 %copy-start = (bf16[2,128,128]{2,1,0:T(8,128)(2,1)S(1)}, bf16[2,128,128]{2,1,0:T(8,128)(2,1)}, u32[]{:S(2)}) copy-start(bf16[2,128,128]{2,1,0:T(8,128)(2,1)} %param.13) | copy-start | bytes 196612
  7.2 76.4 %all-gather.4.cloned.1.call-start = ((), (), s32[]{:S(2)}) async-start(), calls=%async_computation.1 | async-start | bytes 8912896 | tf_op jit(solution)/shard_map/all_gather | solution.py:15
  9.4 173.2 %all-gather.6.cloned.1.call-start = ((), (), s32[]{:S(2)}) async-start(), calls=%async_computation.3 | async-start | bytes 4718592 | tf_op jit(solution)/shard_map/all_gather | solution.py:12
  90.1 15.0 %copy-start.4 = (s32[512]{0:T(512)S(1)}, s32[512]{0:T(512)}, u32[]{:S(2)}) copy-start(s32[512]{0:T(512)} %param.10) | copy-start | bytes 6148
  105.2 154.2 %copy-start.3 = (f32[2,4,128]{2,1,0:T(4,128)S(1)}, f32[2,4,128]{2,1,0:T(4,128)}, u32[]{:S(2)}) copy-start(f32[2,4,128]{2,1,0:T(4,128)} %param.12) | copy-start | bytes 12292
  149.9 0.8 copy-start.1
  150.7 108.0 %reduce-scatter.2.cloned.1.call-start = ((), (), s32[]{:S(2)}) async-start(), calls=%async_computation.2 | async-start | bytes 557056 | tf_op jit(solution)/shard_map/reduce_scatter | solution.py:25
  259.4 0.7 copy-start.2
Sparse Core Ops, SparseCore 0:
  10.2 73.3 all-gather.3
  150.8 31.6 all-gather.5
  186.2 72.4 reduce-scatter.1
